TPU v7x, 256 devices: a whole 4x4x8 slice. The times are simulated.
256 devices in a mesh: seq: 8 (over z), exp: 8 (over x, y_hi), img: 4 (over y_lo, core).
Axes of the slice: x: 4, y: 4 (y_hi: 2, y_lo: 2; y = y_hi * 2 + y_lo), z: 8, core: 2. Of those that a mesh axis runs over, the one named last changes fastest.
Arguments:
- projected: bfloat16 [32, 1024, 3, 1280], P(('img', 'exp'), 'seq'), parts along dimension 0, may hold values from -6 to 6
- residual: bfloat16 [32, 1024, 1280], P(('img', 'exp'), 'seq'), parts along dimension 0, may hold values from -6 to 6
- attn_proj: bfloat16 [1280, 1280], P('seq'), may hold values from -0.15625 to 0.15625
- norm_gain: float32 [1280], replicated, may hold values from 0.5 to 2
- norm_bias: float32 [1280], replicated, may hold values from -3 to 3
- expert_ids: int32 [32, 1024, 1], P(('img', 'exp')), parts along dimension 0, may hold values from 0 to 15; in each aligned block of 128 rows (0 to 127, 128 to 255, ..., all dimensions but the last counted through in order) at most 12 rows name the same one
- expert_up: bfloat16 [16, 1280, 5120], P('exp', None, 'seq'), may hold values from -0.15625 to 0.15625
- expert_down: bfloat16 [16, 5120, 1280], P('exp', 'seq'), may hold values from -0.078125 to 0.078125
Outputs:
- layer_out: bfloat16 [32, 1024, 1280], P(('img', 'exp'), 'seq'), parts along dimension 0
There are 4 independent parts, one for each index of `img`. A program takes and returns all parts, laid end to end along the dimension named above; an argument that names none is the same for every part. Nothing has to cross between parts.
Inputs may be any that keep to these rules, and one draw needn't show every extreme that they name: `expert_ids`: in each sequence, within every aligned block of 128 tokens, no expert is named by more than 12 tokens.
All inputs are finite; a program needn't handle non-finite values.
Results may differ from a plain program's by a relative error of at most 0.015.
Values may be sent and summed in bfloat16 or wider, within the bound.
No kernel may reach another device: no remote copies, remote signals or barrier semaphores. Data moves between devices by JAX's collectives and lax.ppermute only.
A program may use at most 64 MiB of HBM per device.

v0:
```python
import jax
import jax.numpy as jnp
from jax import lax
from jax.sharding import PartitionSpec as P

HEADS = 16
HEAD_DIM = 80


def attend(gathered):
    queries = gathered[:, 0, 0]
    keys_all = gathered[:, 1, 0]
    values = gathered[:, 2, 0]
    length = queries.shape[0]
    span_rows = min(512, length)
    factor = 1.0 / queries.shape[2] ** 0.5

    def one_block(offset):
        query_rows = lax.dynamic_slice_in_dim(queries, offset, span_rows, 0)
        scores = (
            jnp.einsum("qhd,khd->hqk", query_rows, keys_all, preferred_element_type=jnp.float32)
            * factor
        )
        peak = jnp.max(scores, axis=-1, keepdims=True)
        powers = jnp.exp(scores - peak)
        weights = (powers / jnp.sum(powers, axis=-1, keepdims=True)).astype(jnp.bfloat16)
        mixed = jnp.einsum("hqk,khd->qhd", weights, values, preferred_element_type=jnp.float32)
        return mixed.astype(jnp.bfloat16)

    starts = jnp.arange(length // span_rows, dtype=jnp.int32) * span_rows
    blocks = lax.map(one_block, starts)
    return blocks.reshape(length, queries.shape[1], queries.shape[2])


def layer_norm(stream, norm_gain, norm_bias):
    values = stream.astype(jnp.float32)
    centre = jnp.mean(values, axis=-1, keepdims=True)
    centered = values - centre
    variance = jnp.mean(centered * centered, axis=-1, keepdims=True)
    return (centered / jnp.sqrt(variance + 1e-06) * norm_gain + norm_bias).astype(jnp.bfloat16)


def per_device(
    projected, residual, attn_proj, norm_gain, norm_bias, expert_ids, expert_up, expert_down
):
    tok_rows = projected.shape[1]
    model_width = projected.shape[3]
    seq_count = lax.axis_size("seq")
    exp_count = lax.axis_size("exp")
    local_experts = expert_up.shape[0]
    experts = local_experts * exp_count
    cap_dev = 3 * tok_rows // (2 * experts)
    capacity = cap_dev * seq_count
    length = tok_rows * seq_count
    heads_here = HEADS // seq_count
    head_width = heads_here * HEAD_DIM
    regrouped = projected[0].reshape(tok_rows, 3, seq_count, heads_here, HEAD_DIM)
    attended = attend(lax.all_to_all(regrouped, "seq", split_axis=2, concat_axis=0, tiled=True))
    attended = attended.reshape(seq_count, tok_rows, 1, head_width)
    token_heads = lax.all_to_all(attended, "seq", split_axis=0, concat_axis=2, tiled=True).reshape(
        tok_rows, model_width
    )
    projected_sum = jnp.dot(
        token_heads,
        lax.all_gather(attn_proj, "seq", axis=0, tiled=True),
        preferred_element_type=jnp.float32,
    )
    stream_own = residual[0].astype(jnp.float32) + projected_sum
    stream = stream_own.astype(jnp.bfloat16)
    stream_own = stream.astype(jnp.float32)
    normed = layer_norm(stream, norm_gain, norm_bias)
    ids_flat = expert_ids[0, :, 0]
    onehot = (ids_flat[:, None] == jnp.arange(experts, dtype=jnp.int32)[None, :]).astype(jnp.int32)
    blocks = onehot.reshape(seq_count, tok_rows, experts)
    before = jnp.cumsum(blocks, axis=1) - blocks
    order_in_block = jnp.sum(before * blocks, axis=2).reshape(length)
    block_id = jnp.arange(length, dtype=jnp.int32) // tok_rows
    slot_all = ids_flat * capacity + block_id * cap_dev + order_in_block
    normed_all = lax.all_gather(normed, "seq", axis=0, tiled=True)
    buffer = jnp.zeros((experts * capacity, model_width), jnp.bfloat16).at[slot_all].set(normed_all)
    buffer = buffer.reshape(exp_count, local_experts, capacity, model_width)
    arrived = lax.all_to_all(buffer, "exp", split_axis=0, concat_axis=0, tiled=True)
    hidden = jax.nn.gelu(
        jnp.einsum("secd,edf->secf", arrived, expert_up, preferred_element_type=jnp.float32),
        approximate=False,
    ).astype(jnp.bfloat16)
    pieces = jnp.einsum(
        "secf,efd->secd", hidden, expert_down, preferred_element_type=jnp.float32
    ).astype(jnp.bfloat16)
    returned = lax.all_to_all(pieces, "exp", split_axis=0, concat_axis=0, tiled=True).reshape(
        experts * capacity, model_width
    )
    per_token = jnp.take(returned, slot_all, axis=0).astype(jnp.float32)
    expert_out = lax.psum_scatter(
        per_token.astype(jnp.bfloat16), "seq", scatter_dimension=0, tiled=True
    ).astype(jnp.float32)
    return (stream_own + expert_out).astype(jnp.bfloat16)[None]


def solution(mesh):
    return jax.shard_map(
        per_device,
        mesh=mesh,
        in_specs=(
            P(("img", "exp"), "seq", None, None),
            P(("img", "exp"), "seq", None),
            P("seq", None),
            P(),
            P(),
            P(("img", "exp"), None, None),
            P("exp", None, "seq"),
            P("exp", "seq", None),
        ),
        out_specs=P(("img", "exp"), "seq", None),
        check_vma=False,
    )
```

profile of v0, /device:TPU:8, one launch (start us, length us, event | category | flops | bytes accessed | tf_op | source)
XLA Modules:
  0.0 343.8 jit_solution(7028651593634963282)
XLA Ops:
  6.5 0.7 all-gather.3.cloned.1.call-update
  7.3 2.5 copy.32
  9.8 2.2 copy.33
  12.0 8.5 %all-to-all-start = ((bf16[128,3,8,2,80]{0,4,3,1,2:T(8,128)(2,1)}), bf16[128,3,8,2,80]{0,4,3,1,2:T(8,128)(2,1)}, u32[]{:S(2)}, u32[]{:S(2)}) async-start(bf16[128,3,8,2,80]{0,4,3,1,2:T(8,128)(2,1)} %copy.33), calls=%async_computation | async-start | bytes 1966080 | tf_op jit(solution)/shard_map/all_to_all | solution.py:58
  20.5 37.9 %all-to-all-done = bf16[128,3,8,2,80]{0,4,3,1,2:T(8,128)(2,1)} async-done(((bf16[128,3,8,2,80]{0,4,3,1,2:T(8,128)(2,1)}), bf16[128,3,8,2,80]{0,4,3,1,2:T(8,128)(2,1)}, u32[]{:S(2)}, u32[]{:S(2)}) %all-to-all-start) | async-done | bytes 983072 | tf_op jit(solution)/shard_map/all_to_all | solution.py:58
  58.4 1.3 copy_bitcast_fusion
  59.7 1.0 slice_bitcast_fusion
  60.7 22.1 %while.10 = (s32[]{:T(128)}, bf16[2,512,2,80]{1,3,2,0:T(8,128)(2,1)}, s32[2]{0:T(128)S(1)}, bf16[1024,2,80]{0,2,1:T(8,128)(2,1)}, bf16[1024,2,80]{0,2,1:T(8,128)...) while((s32[]{:T(128)}, bf16[2,512,2,80]{1,3,2,0:T(8,128)(2,1)}, ...), condition=%wide.region_3.4_spmd, body=%wide.region_0.3_spmd.sunk | while | flops 340870144 | bytes 9380495 | solution.py:31
  60.7 0.7 dynamic_slice.22
  63.5 4.6 %fusion.154 = (f32[2,512]{1,0:T(2,128)S(1)}, f32[2,512,1024]{2,1,0:T(8,128)}) fusion(bf16[1024,2,80]{0,2,1:T(8,128)(2,1)} %get-tuple-element.120, bf16[1024,2,80]{0,2,1:T(8,128)(2,1)} %get-tuple-element.119, s32[]{:T(128)S(6)} %select_n.70), kind=kOutput, calls=%fused_computation.154.clone.1 | convolution fusion | flops 170918912 | bytes 4689924 | tf_op jit(solution)/shard_map/while/body/eval_jaxpr/sub | solution.py:25
  68.0 3.8 %fusion.155 = bf16[2,512,2,80]{1,3,2,0:T(8,128)(2,1)} fusion(bf16[2,512,2,80]{1,3,2,0:T(8,128)(2,1)} %get-tuple-element.108, s32[]{:T(128)} %get-tuple-element.107, bf16[1024,2,80]{0,2,1:T(8,128)(2,1)} %get-tuple-element.121, f32[2,512,1024]{2,1,0:T(8,128)} %get-tuple-element.96, f32[2,512]{1,0:T(2,128)S(1)} %get-tuple-element.97), kind=kOutput, calls=%fused_computation.11.clone.1 | convolution fusion | flops 169951232 | bytes 4690432 | tf_op jit(solution)/shard_map/while/body/eval_jaxpr/hqk,khd->qhd/dot_general | solution.py:27
  71.8 0.7 dynamic_slice.22
  74.6 4.5 %fusion.154 = (f32[2,512]{1,0:T(2,128)S(1)}, f32[2,512,1024]{2,1,0:T(8,128)}) fusion(bf16[1024,2,80]{0,2,1:T(8,128)(2,1)} %get-tuple-element.120, bf16[1024,2,80]{0,2,1:T(8,128)(2,1)} %get-tuple-element.119, s32[]{:T(128)S(6)} %select_n.70), kind=kOutput, calls=%fused_computation.154.clone.1 | convolution fusion | flops 170918912 | bytes 4689924 | tf_op jit(solution)/shard_map/while/body/eval_jaxpr/sub | solution.py:25
  79.1 3.7 %fusion.155 = bf16[2,512,2,80]{1,3,2,0:T(8,128)(2,1)} fusion(bf16[2,512,2,80]{1,3,2,0:T(8,128)(2,1)} %get-tuple-element.108, s32[]{:T(128)} %get-tuple-element.107, bf16[1024,2,80]{0,2,1:T(8,128)(2,1)} %get-tuple-element.121, f32[2,512,1024]{2,1,0:T(8,128)} %get-tuple-element.96, f32[2,512]{1,0:T(2,128)S(1)} %get-tuple-element.97), kind=kOutput, calls=%fused_computation.11.clone.1 | convolution fusion | flops 169951232 | bytes 4690432 | tf_op jit(solution)/shard_map/while/body/eval_jaxpr/hqk,khd->qhd/dot_general | solution.py:27
  82.8 2.0 copy.35
  84.9 1.9 reshape_reshape.3
  86.8 1.0 copy.36
  87.8 16.6 %all_to_all.43 = bf16[8,128,1,160]{1,3,2,0:T(8,128)(2,1)} all-to-all(bf16[8,128,1,160]{1,3,2,0:T(8,128)(2,1)S(1)} %copy.36), channel_id=1, replica_groups=mesh['seq'=8,'exp'=8,'img'=4] {'seq'}, dimensions={0} | all-to-all | bytes 655360 | tf_op jit(solution)/shard_map/all_to_all | solution.py:60
  104.4 2.8 fusion.139
  108.1 0.9 add_convert_fusion.1
  109.1 2.5 select_reduce_fusion
  111.7 35.8 %all-gather.5.cloned.1.call-done = bf16[1024,1280]{1,0:T(8,128)(2,1)} async-done(((bf16[128,1280]{1,0:T(8,128)(2,1)}), bf16[1024,1280]{1,0:T(8,128)(2,1)}) %all-gather.5.cloned.1.call-update) | async-done | bytes 2621456 | tf_op jit(solution)/shard_map/all_gather | solution.py:79
  147.5 8.6 %scatter_custom_fusion = bf16[1536,1280]{1,0:T(8,128)(2,1)} fusion(s32[1024]{0:T(1024)S(1)} %bitcast.147, bf16[1024,1280]{1,0:T(8,128)(2,1)} %all-gather.5.cloned.1.call-done, bf16[]{:T(256)} %constant.31.clone.1), kind=kCustom, calls=%fused_computation.83 | custom fusion | bytes 3932672 | tf_op jit(solution)/shard_map/scatter | solution.py:80
  156.1 50.5 %all_to_all.44 = bf16[8,2,96,1280]{3,2,1,0:T(8,128)(2,1)} all-to-all(bf16[8,2,96,1280]{3,2,1,0:T(8,128)(2,1)} %bitcast.142), channel_id=1, replica_groups=mesh['seq'=8,'exp'=8,'img'=4] {'exp'}, dimensions={0} | all-to-all | bytes 7864320 | tf_op jit(solution)/shard_map/all_to_all | solution.py:82
  206.6 17.1 %fusion.43 = bf16[8,2,96,1280]{3,2,0,1:T(8,128)(2,1)} fusion(bf16[2,640,1280]{2,1,0:T(8,128)(2,1)S(1)} %copy-done, bf16[8,2,96,1280]{3,2,1,0:T(8,128)(2,1)} %all_to_all.44, bf16[2,1280,640]{2,1,0:T(8,128)(2,1)} %param.16), kind=kOutput, calls=%fused_computation.46 | convolution fusion | flops 5099028480 | bytes 14417920 | tf_op jit(solution)/shard_map/secf,efd->secd/dot_general | solution.py:87
  223.7 4.3 %copy.41 = bf16[8,2,96,1280]{3,2,1,0:T(8,128)(2,1)} copy(bf16[8,2,96,1280]{3,2,0,1:T(8,128)(2,1)} %fusion.43) | data formatting | bytes 7864320 | tf_op jit(solution)/shard_map/convert_element_type | solution.py:89
  228.0 4.5 %all-to-all-start.3 = ((bf16[8,2,96,1280]{3,2,1,0:T(8,128)(2,1)}), bf16[8,2,96,1280]{3,2,1,0:T(8,128)(2,1)}, u32[]{:S(2)}, u32[]{:S(2)}) async-start(bf16[8,2,96,1280]{3,2,1,0:T(8,128)(2,1)} %copy.41), calls=%async_computation.3 | async-start | bytes 7864320 | tf_op jit(solution)/shard_map/all_to_all | solution.py:90
  232.6 50.5 %all-to-all-done.3 = bf16[8,2,96,1280]{3,2,1,0:T(8,128)(2,1)} async-done(((bf16[8,2,96,1280]{3,2,1,0:T(8,128)(2,1)}), bf16[8,2,96,1280]{3,2,1,0:T(8,128)(2,1)}, u32[]{:S(2)}, u32[]{:S(2)}) %all-to-all-start.3) | async-done | bytes 3932192 | tf_op jit(solution)/shard_map/all_to_all | solution.py:90
  283.1 9.2 %gather_fusion = bf16[1024,1280]{1,0:T(8,128)(2,1)} fusion(bf16[1536,1280]{1,0:T(8,128)(2,1)} %bitcast.27, s32[1024]{0:T(1024)S(1)} %broadcast_clamp_fusion), kind=kCustom, calls=%fused_computation | custom fusion | bytes 5246976 | tf_op jit(solution)/shard_map/jit(_take)/gather | solution.py:93
  292.3 3.5 %broadcast_select_fusion = bf16[1024,1280]{1,0:T(8,128)(2,1)} fusion(bf16[1024,1280]{1,0:T(8,128)(2,1)} %gather_fusion, pred[1024]{0:T(1024)(128)(4,1)S(1)} %compare_and_fusion), kind=kLoop, calls=%fused_computation.49 | loop fusion | flops 1310720 | bytes 5243904 | tf_op jit(solution)/shard_map/jit(_take)/select_n | solution.py:93
  295.9 39.4 %reduce-scatter.2.cloned.1.call-done = bf16[128,1280]{1,0:T(8,128)(2,1)} async-done(((bf16[1024,1280]{1,0:T(8,128)(2,1)}), bf16[128,1280]{1,0:T(8,128)(2,1)}) %reduce-scatter.2.cloned.1.call-update) | async-done | bytes 327696 | tf_op jit(solution)/shard_map/reduce_scatter | solution.py:94
  335.3 1.9 fusion.93
  (27 shorter events, 1.2 us)
Async XLA Ops:
  6.5 200.1 %copy-start = (bf16[2,640,1280]{2,1,0:T(8,128)(2,1)S(1)}, bf16[2,640,1280]{2,1,0:T(8,128)(2,1)}, u32[]{:S(2)}) copy-start(bf16[2,640,1280]{2,1,0:T(8,128)(2,1)} %param.17) | copy-start | bytes 9830404
  6.5 97.9 %all-gather.3.cloned.1.call-start = ((), (), s32[]{:S(2)}) async-start(), calls=%async_computation.5 | async-start | bytes 3686400 | tf_op jit(solution)/shard_map/all_gather | solution.py:65
  12.0 46.4 %all-to-all-start = ((bf16[128,3,8,2,80]{0,4,3,1,2:T(8,128)(2,1)}), bf16[128,3,8,2,80]{0,4,3,1,2:T(8,128)(2,1)}, u32[]{:S(2)}, u32[]{:S(2)}) async-start(bf16[128,3,8,2,80]{0,4,3,1,2:T(8,128)(2,1)} %copy.33), calls=%async_computation | async-start | bytes 1966080 | tf_op jit(solution)/shard_map/all_to_all | solution.py:58
  20.4 127.1 %all-gather.5.cloned.1.call-start = ((), (), s32[]{:S(2)}) async-start(), calls=%async_computation.6 | async-start | bytes 2949120 | tf_op jit(solution)/shard_map/all_gather | solution.py:79
  82.8 25.2 %copy-start.3 = (f32[1280]{0:T(1024)S(1)}, f32[1280]{0:T(1024)}, u32[]{:S(2)}) copy-start(f32[1280]{0:T(1024)} %param.14) | copy-start | bytes 15364
  82.8 25.3 %copy-start.4 = (f32[1280]{0:T(1024)S(1)}, f32[1280]{0:T(1024)}, u32[]{:S(2)}) copy-start(f32[1280]{0:T(1024)} %param.13) | copy-start | bytes 15364
  86.8 22.2 %copy-start.2 = (s32[1,1024,1]{1,2,0:T(1,128)S(1)}, s32[1,1024,1]{1,2,0:T(1,128)}, u32[]{:S(2)}) copy-start(s32[1,1024,1]{1,2,0:T(1,128)} %param.15) | copy-start | bytes 12292
  107.2 0.9 copy-start.1
  228.0 55.1 %all-to-all-start.3 = ((bf16[8,2,96,1280]{3,2,1,0:T(8,128)(2,1)}), bf16[8,2,96,1280]{3,2,1,0:T(8,128)(2,1)}, u32[]{:S(2)}, u32[]{:S(2)}) async-start(bf16[8,2,96,1280]{3,2,1,0:T(8,128)(2,1)} %copy.41), calls=%async_computation.3 | async-start | bytes 7864320 | tf_op jit(solution)/shard_map/all_to_all | solution.py:90
  232.5 102.8 %reduce-scatter.2.cloned.1.call-start = ((), (), s32[]{:S(2)}) async-start(), calls=%async_computation.7 | async-start | bytes 2949120 | tf_op jit(solution)/shard_map/reduce_scatter | solution.py:94
Sparse Core Ops, SparseCore 0:
  9.1 67.2 all-gather.2
  109.1 38.3 all-gather.4
  296.0 39.2 reduce-scatter.1
where the time goes:
time: 344 us
  waiting for transfers between devices  164 us (48%)
  blocking collectives  67.1 us (20%)
  matrix products  36.5 us (11%)
  local copies, waits for them, and re-layouts  36.3 us (11%)
  between operations  13.2 us (4%)
  starting transfers between devices  13.1 us (4%)
  other arithmetic  9.21 us (3%)
  loops' own time  4.15 us (1%)
    all_to_all x1, blocking collectives, per_device(): lax.all_to_all(buffer, 'exp', split_axis=0, concat_axis=0, tiled=True)  50.5 us
    all_to_all x1, waiting for transfers between devices, per_device(): lax.all_to_all(pieces, 'exp', split_axis=0, concat_axis=0, tiled=True)  50.5 us
    reduce_scatter x1, waiting for transfers between devices, per_device(): lax.psum_scatter(per_token.astype(jnp.bfloat16), 'seq', scatter_dimension...  39.4 us
    all_to_all x1, waiting for transfers between devices, per_device(): lax.all_to_all(regrouped, 'seq', split_axis=2, concat_axis=0, tiled=True)  37.9 us
    all_gather x1, waiting for transfers between devices, per_device(): normed_all = lax.all_gather(normed, 'seq', axis=0, tiled=True)  35.8 us
    dot_general x1, matrix products, per_device(): jnp.einsum('secf,efd->secd', hidden, expert_down, preferred_element_type=...  17.1 us
    all_to_all x1, blocking collectives, per_device(): lax.all_to_all(attended, 'seq', split_axis=0, concat_axis=2, tiled=True)  16.6 us
    gather x1, local copies, waits for them, and re-layouts, per_device(): per_token = jnp.take(returned, slot_all, axis=0).astype(jnp.float32)  9.22 us
  transfers between devices with their start and end apart: 5, of which 4 were waited for; matrix products, arithmetic and copies ran while one was open for 10% of the time, Pallas kernels for 0%

commit v1 on v0

--- a/solution.py
+++ b/solution.py
@@ -5,6 +5,13 @@
 
 HEADS = 16
 HEAD_DIM = 80
+
+
+def swapped_in(x, axis, dim):
+    count = lax.axis_size(axis)
+    blocks = jnp.stack([x for _ in range(count)])
+    blocks = lax.all_to_all(blocks, axis, split_axis=0, concat_axis=0)
+    return jnp.concatenate(blocks, axis=dim)
 
 
 def attend(gathered):
@@ -76,7 +83,7 @@
     order_in_block = jnp.sum(before * blocks, axis=2).reshape(length)
     block_id = jnp.arange(length, dtype=jnp.int32) // tok_rows
     slot_all = ids_flat * capacity + block_id * cap_dev + order_in_block
-    normed_all = lax.all_gather(normed, "seq", axis=0, tiled=True)
+    normed_all = swapped_in(normed, "seq", 0)
     buffer = jnp.zeros((experts * capacity, model_width), jnp.bfloat16).at[slot_all].set(normed_all)
     buffer = buffer.reshape(exp_count, local_experts, capacity, model_width)
     arrived = lax.all_to_all(buffer, "exp", split_axis=0, concat_axis=0, tiled=True)

time: 344 us -> 379 us (1.10)
  waiting for transfers between devices: 164 us -> 190 us
  starting transfers between devices: 13.1 us -> 17.4 us
    all_to_all x0 -> x1, waiting for transfers between devices: none -> 59.3 us  [swapped_in(): blocks = lax.all_to_all(blocks, axis, split_axis=0, concat_axis=0)]
    all_gather x1 -> x0, waiting for transfers between devices: 35.8 us -> none  [per_device(): normed_all = lax.all_gather(normed, 'seq', axis=0, tiled=True)]
    all_to_all x0 -> x1, starting transfers between devices: none -> 4.39 us  [swapped_in(): blocks = lax.all_to_all(blocks, axis, split_axis=0, concat_axis=0)]
    all_to_all x1, waiting for transfers between devices: 50.5 us -> 54.5 us  [per_device(): lax.all_to_all(pieces, 'exp', split_axis=0, concat_axis=0, tiled=True)]
  transfers between devices with their start and end apart: 5 -> 5, of which waited for: 4 -> 4; matrix products, arithmetic and copies ran while one was open for 10% -> 9% of each run, Pallas kernels for 0% -> 0%
where the time goes in v1:
time: 379 us
  waiting for transfers between devices  190 us (50%)
  blocking collectives  70.8 us (19%)
  local copies, waits for them, and re-layouts  37.9 us (10%)
  matrix products  36.5 us (10%)
  starting transfers between devices  17.4 us (5%)
  between operations  13.5 us (4%)
  other arithmetic  8.49 us (2%)
  loops' own time  4.15 us (1%)
    all_to_all x1, waiting for transfers between devices, swapped_in(): blocks = lax.all_to_all(blocks, axis, split_axis=0, concat_axis=0)  59.3 us
    all_to_all x1, waiting for transfers between devices, per_device(): lax.all_to_all(pieces, 'exp', split_axis=0, concat_axis=0, tiled=True)  54.5 us
    all_to_all x1, blocking collectives, per_device(): lax.all_to_all(buffer, 'exp', split_axis=0, concat_axis=0, tiled=True)  54.2 us
    all_to_all x1, waiting for transfers between devices, per_device(): lax.all_to_all(regrouped, 'seq', split_axis=2, concat_axis=0, tiled=True)  37.9 us
    reduce_scatter x1, waiting for transfers between devices, per_device(): lax.psum_scatter(per_token.astype(jnp.bfloat16), 'seq', scatter_dimension...  37.4 us
    dot_general x1, matrix products, per_device(): jnp.einsum('secf,efd->secd', hidden, expert_down, preferred_element_type=...  17.1 us
    all_to_all x1, blocking collectives, per_device(): lax.all_to_all(attended, 'seq', split_axis=0, concat_axis=2, tiled=True)  16.6 us
    gather x1, local copies, waits for them, and re-layouts, per_device(): per_token = jnp.take(returned, slot_all, axis=0).astype(jnp.float32)  9.22 us
  transfers between devices with their start and end apart: 5, of which 4 were waited for; matrix products, arithmetic and copies ran while one was open for 9% of the time, Pallas kernels for 0%

profile of v1, /device:TPU:8, one launch (start us, length us, event | category | flops | bytes accessed | tf_op | source)
XLA Modules:
  0.0 378.6 jit_solution(4055620462331409286)
XLA Ops:
  6.5 0.7 all-gather.2.cloned.1.call-update
  7.3 2.5 copy.32
  9.8 2.2 copy.33
  12.0 8.5 %all-to-all-start = ((bf16[128,3,8,2,80]{0,4,3,1,2:T(8,128)(2,1)}), bf16[128,3,8,2,80]{0,4,3,1,2:T(8,128)(2,1)}, u32[]{:S(2)}, u32[]{:S(2)}) async-start(bf16[128,3,8,2,80]{0,4,3,1,2:T(8,128)(2,1)} %copy.33), calls=%async_computation | async-start | bytes 1966080 | tf_op jit(solution)/shard_map/all_to_all | solution.py:65
  20.4 37.9 %all-to-all-done = bf16[128,3,8,2,80]{0,4,3,1,2:T(8,128)(2,1)} async-done(((bf16[128,3,8,2,80]{0,4,3,1,2:T(8,128)(2,1)}), bf16[128,3,8,2,80]{0,4,3,1,2:T(8,128)(2,1)}, u32[]{:S(2)}, u32[]{:S(2)}) %all-to-all-start) | async-done | bytes 983072 | tf_op jit(solution)/shard_map/all_to_all | solution.py:65
  58.4 1.3 copy_bitcast_fusion
  59.7 1.0 slice_bitcast_fusion
  60.7 22.1 %while.10 = (s32[]{:T(128)}, bf16[2,512,2,80]{1,3,2,0:T(8,128)(2,1)}, s32[2]{0:T(128)S(1)}, bf16[1024,2,80]{0,2,1:T(8,128)(2,1)}, bf16[1024,2,80]{0,2,1:T(8,128)...) while((s32[]{:T(128)}, bf16[2,512,2,80]{1,3,2,0:T(8,128)(2,1)}, ...), condition=%wide.region_3.4_spmd, body=%wide.region_0.3_spmd.sunk | while | flops 340870144 | bytes 9380495 | solution.py:38
  63.5 4.6 %fusion.154 = (f32[2,512]{1,0:T(2,128)S(1)}, f32[2,512,1024]{2,1,0:T(8,128)}) fusion(bf16[1024,2,80]{0,2,1:T(8,128)(2,1)} %get-tuple-element.120, bf16[1024,2,80]{0,2,1:T(8,128)(2,1)} %get-tuple-element.119, s32[]{:T(128)S(6)} %select_n.70), kind=kOutput, calls=%fused_computation.154.clone.1 | convolution fusion | flops 170918912 | bytes 4689924 | tf_op jit(solution)/shard_map/while/body/eval_jaxpr/sub | solution.py:32
  68.0 3.8 fusion.155
  71.8 0.7 dynamic_slice.22
  74.6 4.5 %fusion.154 = (f32[2,512]{1,0:T(2,128)S(1)}, f32[2,512,1024]{2,1,0:T(8,128)}) fusion(bf16[1024,2,80]{0,2,1:T(8,128)(2,1)} %get-tuple-element.120, bf16[1024,2,80]{0,2,1:T(8,128)(2,1)} %get-tuple-element.119, s32[]{:T(128)S(6)} %select_n.70), kind=kOutput, calls=%fused_computation.154.clone.1 | convolution fusion | flops 170918912 | bytes 4689924 | tf_op jit(solution)/shard_map/while/body/eval_jaxpr/sub | solution.py:32
  79.1 3.7 fusion.155
  82.8 2.0 copy.35
  84.9 1.9 reshape_reshape.3
  86.8 1.0 copy.36
  87.8 16.6 %all_to_all.48 = bf16[8,128,1,160]{1,3,2,0:T(8,128)(2,1)} all-to-all(bf16[8,128,1,160]{1,3,2,0:T(8,128)(2,1)S(1)} %copy.36), channel_id=1, replica_groups=mesh['seq'=8,'exp'=8,'img'=4] {'seq'}, dimensions={0} | all-to-all | bytes 655360 | tf_op jit(solution)/shard_map/all_to_all | solution.py:67
  104.4 2.8 fusion.139
  108.3 1.7 stack.2
  109.9 4.4 %all-to-all-start.2 = ((bf16[8,128,1280]{2,1,0:T(8,128)(2,1)}), bf16[8,128,1280]{2,1,0:T(8,128)(2,1)}, u32[]{:S(2)}, u32[]{:S(2)}) async-start(bf16[8,128,1280]{2,1,0:T(8,128)(2,1)} %stack.2), calls=%async_computation.2 | async-start | bytes 5242880 | tf_op jit(solution)/shard_map/all_to_all | solution.py:13
  114.4 2.5 select_reduce_fusion
  117.1 59.3 %all-to-all-done.2 = bf16[8,128,1280]{2,1,0:T(8,128)(2,1)} async-done(((bf16[8,128,1280]{2,1,0:T(8,128)(2,1)}), bf16[8,128,1280]{2,1,0:T(8,128)(2,1)}, u32[]{:S(2)}, u32[]{:S(2)}) %all-to-all-start.2) | async-done | bytes 2621472 | tf_op jit(solution)/shard_map/all_to_all | solution.py:13
  176.3 8.6 %scatter_custom_fusion = bf16[1536,1280]{1,0:T(8,128)(2,1)} fusion(s32[1024]{0:T(1024)S(1)} %bitcast.148, bf16[1024,1280]{1,0:T(8,128)(2,1)} %bitcast.19, bf16[]{:T(256)} %constant.31.clone.1), kind=kCustom, calls=%fused_computation.83 | custom fusion | bytes 3932672 | tf_op jit(solution)/shard_map/scatter | solution.py:87
  184.9 54.2 %all_to_all.49 = bf16[8,2,96,1280]{3,2,1,0:T(8,128)(2,1)} all-to-all(bf16[8,2,96,1280]{3,2,1,0:T(8,128)(2,1)} %bitcast.143), channel_id=1, replica_groups=mesh['seq'=8,'exp'=8,'img'=4] {'exp'}, dimensions={0} | all-to-all | bytes 7864320 | tf_op jit(solution)/shard_map/all_to_all | solution.py:89
  239.1 17.1 %fusion.43 = bf16[8,2,96,1280]{3,2,0,1:T(8,128)(2,1)} fusion(bf16[2,640,1280]{2,1,0:T(8,128)(2,1)S(1)} %copy-done, bf16[8,2,96,1280]{3,2,1,0:T(8,128)(2,1)} %all_to_all.49, bf16[2,1280,640]{2,1,0:T(8,128)(2,1)} %param.16), kind=kOutput, calls=%fused_computation.46 | convolution fusion | flops 5099028480 | bytes 14417920 | tf_op jit(solution)/shard_map/secf,efd->secd/dot_general | solution.py:94
  256.2 4.3 %copy.41 = bf16[8,2,96,1280]{3,2,1,0:T(8,128)(2,1)} copy(bf16[8,2,96,1280]{3,2,0,1:T(8,128)(2,1)} %fusion.43) | data formatting | bytes 7864320 | tf_op jit(solution)/shard_map/convert_element_type | solution.py:96
  260.5 4.5 %all-to-all-start.4 = ((bf16[8,2,96,1280]{3,2,1,0:T(8,128)(2,1)}), bf16[8,2,96,1280]{3,2,1,0:T(8,128)(2,1)}, u32[]{:S(2)}, u32[]{:S(2)}) async-start(bf16[8,2,96,1280]{3,2,1,0:T(8,128)(2,1)} %copy.41), calls=%async_computation.4 | async-start | bytes 7864320 | tf_op jit(solution)/shard_map/all_to_all | solution.py:97
  265.1 54.5 %all-to-all-done.4 = bf16[8,2,96,1280]{3,2,1,0:T(8,128)(2,1)} async-done(((bf16[8,2,96,1280]{3,2,1,0:T(8,128)(2,1)}), bf16[8,2,96,1280]{3,2,1,0:T(8,128)(2,1)}, u32[]{:S(2)}, u32[]{:S(2)}) %all-to-all-start.4) | async-done | bytes 3932192 | tf_op jit(solution)/shard_map/all_to_all | solution.py:97
  319.7 9.2 %gather_fusion = bf16[1024,1280]{1,0:T(8,128)(2,1)} fusion(bf16[1536,1280]{1,0:T(8,128)(2,1)} %bitcast.28, s32[1024]{0:T(1024)S(1)} %broadcast_clamp_fusion), kind=kCustom, calls=%fused_computation | custom fusion | bytes 5246976 | tf_op jit(solution)/shard_map/jit(_take)/gather | solution.py:100
  328.9 3.5 broadcast_select_fusion
  332.5 37.4 %reduce-scatter.2.cloned.1.call-done = bf16[128,1280]{1,0:T(8,128)(2,1)} async-done(((bf16[1024,1280]{1,0:T(8,128)(2,1)}), bf16[128,1280]{1,0:T(8,128)(2,1)}) %reduce-scatter.2.cloned.1.call-update) | async-done | bytes 327696 | tf_op jit(solution)/shard_map/reduce_scatter | solution.py:101
  369.8 1.9 fusion.93
  (27 shorter events, 2.0 us)
Async XLA Ops:
  6.5 232.6 %copy-start = (bf16[2,640,1280]{2,1,0:T(8,128)(2,1)S(1)}, bf16[2,640,1280]{2,1,0:T(8,128)(2,1)}, u32[]{:S(2)}) copy-start(bf16[2,640,1280]{2,1,0:T(8,128)(2,1)} %param.17) | copy-start | bytes 9830404
  6.5 97.8 %all-gather.2.cloned.1.call-start = ((), (), s32[]{:S(2)}) async-start(), calls=%async_computation.6 | async-start | bytes 3686400 | tf_op jit(solution)/shard_map/all_gather | solution.py:72
  12.0 46.4 %all-to-all-start = ((bf16[128,3,8,2,80]{0,4,3,1,2:T(8,128)(2,1)}), bf16[128,3,8,2,80]{0,4,3,1,2:T(8,128)(2,1)}, u32[]{:S(2)}, u32[]{:S(2)}) async-start(bf16[128,3,8,2,80]{0,4,3,1,2:T(8,128)(2,1)} %copy.33), calls=%async_computation | async-start | bytes 1966080 | tf_op jit(solution)/shard_map/all_to_all | solution.py:65
  82.8 25.2 %copy-start.3 = (f32[1280]{0:T(1024)S(1)}, f32[1280]{0:T(1024)}, u32[]{:S(2)}) copy-start(f32[1280]{0:T(1024)} %param.14) | copy-start | bytes 15364
  82.8 25.2 %copy-start.4 = (f32[1280]{0:T(1024)S(1)}, f32[1280]{0:T(1024)}, u32[]{:S(2)}) copy-start(f32[1280]{0:T(1024)} %param.13) | copy-start | bytes 15364
  107.2 0.9 copy-start.1
  108.2 6.1 %copy-start.2 = (s32[1,1024,1]{1,2,0:T(1,128)S(1)}, s32[1,1024,1]{1,2,0:T(1,128)}, u32[]{:S(2)}) copy-start(s32[1,1024,1]{1,2,0:T(1,128)} %param.15) | copy-start | bytes 12292
  109.9 66.4 %all-to-all-start.2 = ((bf16[8,128,1280]{2,1,0:T(8,128)(2,1)}), bf16[8,128,1280]{2,1,0:T(8,128)(2,1)}, u32[]{:S(2)}, u32[]{:S(2)}) async-start(bf16[8,128,1280]{2,1,0:T(8,128)(2,1)} %stack.2), calls=%async_computation.2 | async-start | bytes 5242880 | tf_op jit(solution)/shard_map/all_to_all | solution.py:13
  260.5 59.2 %all-to-all-start.4 = ((bf16[8,2,96,1280]{3,2,1,0:T(8,128)(2,1)}), bf16[8,2,96,1280]{3,2,1,0:T(8,128)(2,1)}, u32[]{:S(2)}, u32[]{:S(2)}) async-start(bf16[8,2,96,1280]{3,2,1,0:T(8,128)(2,1)} %copy.41), calls=%async_computation.4 | async-start | bytes 7864320 | tf_op jit(solution)/shard_map/all_to_all | solution.py:97
  265.0 104.8 %reduce-scatter.2.cloned.1.call-start = ((), (), s32[]{:S(2)}) async-start(), calls=%async_computation.7 | async-start | bytes 2949120 | tf_op jit(solution)/shard_map/reduce_scatter | solution.py:101
Sparse Core Ops, SparseCore 0:
  9.1 67.2 all-gather.1
  332.6 37.1 reduce-scatter.1
